TPU v7x, 256 devices: a whole 4x4x8 slice. The times are simulated.
256 devices in a mesh: svc: 32 (over y_lo, z, core), tm: 8 (over y_hi, x).
Axes of the slice: x: 4, y: 4 (y_hi: 2, y_lo: 2; y = y_hi * 2 + y_lo), z: 8, core: 2. Of those that a mesh axis runs over, the one named last changes fastest.
Arguments:
- metrics: bfloat16 [8192, 4096], P('svc', 'tm'), may hold values from -15 to 15
- band_starts: int32 [4], replicated, may hold values from 1 to 2015
Outputs:
- cross: bfloat16 [4, 2, 8192, 8192], P(None, None, 'svc', 'tm')
- coherence: float32 [4, 8192, 8192], P(None, 'svc', 'tm')
Inputs may be any that keep to these rules, and one draw needn't show every extreme that they name: `band_starts`: each band covers 32 consecutive bins starting at its entry.
All inputs are finite; a program needn't handle non-finite values.
Results may differ from a plain program's by a relative error of at most 0.0066.
Values may be sent and summed in bfloat16 or wider, within the bound.
No kernel may reach another device: no remote copies, remote signals or barrier semaphores. Data moves between devices by JAX's collectives and lax.ppermute only.
A program may use at most 64 MiB of HBM per device.

v0:
```python
import jax
import jax.numpy as jnp
from jax import lax
from jax.sharding import PartitionSpec as P

TLEN = 4096
BANDS = 4
BINS = 32
epsilon = 1e-06


def make_table(minutes, band_starts):
    offsets = jnp.arange(BINS, dtype=jnp.int32)
    freqs = band_starts[:, None] + offsets[None, :]
    phase_index = minutes[:, None, None] * freqs[None, :, :] % TLEN
    phases = 2.0 * jnp.pi / TLEN * phase_index.astype(jnp.float32)
    norm = 1.0 / jnp.sqrt(jnp.float32(TLEN))
    stacked = jnp.stack([jnp.cos(phases) * norm, -jnp.sin(phases) * norm], axis=2)
    return stacked.reshape(minutes.shape[0], BANDS * 2 * BINS).astype(jnp.bfloat16)


def band_products(row_spec, col_spec):
    swapped = jnp.concatenate([row_spec[:, BINS:], -row_spec[:, :BINS]], axis=1)
    dims = (((1,), (1,)), ((), ()))
    real_part = lax.dot_general(row_spec, col_spec, dims, preferred_element_type=jnp.float32) / BINS
    imag_part = lax.dot_general(swapped, col_spec, dims, preferred_element_type=jnp.float32) / BINS
    row_power = jnp.sum(jnp.square(row_spec.astype(jnp.float32)), axis=1) / BINS
    col_power = jnp.sum(jnp.square(col_spec.astype(jnp.float32)), axis=1) / BINS
    coherence = (real_part * real_part + imag_part * imag_part) / (
        (row_power[:, None] + epsilon) * (col_power[None, :] + epsilon)
    )
    cross = jnp.stack([real_part, imag_part], axis=0).astype(jnp.bfloat16)
    return (cross, coherence)


def body(metrics, band_starts):
    row_count = metrics.shape[0]
    local_minutes = metrics.shape[1]
    time_index = lax.axis_index("tm")
    minutes = time_index * local_minutes + jnp.arange(local_minutes, dtype=jnp.int32)
    dft_table = make_table(minutes, band_starts)
    partial_value = jnp.dot(metrics, dft_table, preferred_element_type=jnp.float32)
    spectra = lax.psum(partial_value, "tm").astype(jnp.bfloat16)
    owners = lax.axis_size("svc") // lax.axis_size("tm")
    col_count = row_count * owners
    gathered = lax.all_gather(spectra, "svc", axis=0, tiled=True)
    columns_panel = lax.dynamic_slice_in_dim(gathered, time_index * col_count, col_count, 0)
    cross_list = []
    coherence_list = []
    for band in range(BANDS):
        offset = band * 2 * BINS
        row_spec = spectra[:, offset : offset + 2 * BINS]
        col_spec = columns_panel[:, offset : offset + 2 * BINS]
        cross, coherence = band_products(row_spec, col_spec)
        cross_list.append(cross)
        coherence_list.append(coherence)
    return (jnp.stack(cross_list, axis=0), jnp.stack(coherence_list, axis=0))


def solution(mesh):
    return jax.shard_map(
        body,
        mesh=mesh,
        in_specs=(P("svc", "tm"), P()),
        out_specs=(P(None, None, "svc", "tm"), P(None, "svc", "tm")),
        check_vma=False,
    )
```

profile of v0, /device:TPU:1, one launch (start us, length us, event | category | flops | bytes accessed | tf_op | source)
XLA Modules:
  0.0 150.9 jit_solution(4337779228758525286)
XLA Ops:
  7.2 0.0 copy-start
  7.2 0.0 all-gather.2.cloned.1.call-start
  7.2 0.8 iota_add_fusion
  8.0 1.2 multiply_convert_fusion.1
  9.3 0.0 copy-done
  9.3 0.3 convolution_bitcast_fusion
  9.5 38.9 %all-reduce.1 = bf16[256,256]{0,1:T(8,128)(2,1)} all-reduce(f32[256,256]{0,1:T(8,128)S(1)} %convolution_bitcast_fusion), channel_id=1, replica_groups=mesh['svc'=32,'tm'=8] {'tm'}, use_global_device_ids=true, to_apply=%region_0.1 | all-reduce | flops 65536 | bytes 393216 | tf_op jit(solution)/shard_map/psum | solution.py:43
  48.5 0.0 copy-start.1
  48.5 0.0 all-gather.2.cloned.1.call-update
  48.5 0.9 multiply_reduce_fusion.7
  49.4 0.9 fusion.33
  50.3 77.2 %all-gather.2.cloned.1.call-done = bf16[8192,256]{0,1:T(8,128)(2,1)} async-done(((bf16[256,256]{0,1:T(8,128)(2,1)}), bf16[8192,256]{0,1:T(8,128)(2,1)}) %all-gather.2.cloned.1.call-update) | async-done | bytes 4194320 | tf_op jit(solution)/shard_map/all_gather | solution.py:46
  127.4 1.2 multiply_reduce_fusion.3
  128.7 1.2 convolution_multiply_fusion
  129.9 1.2 convolution_multiply_fusion.2
  131.2 1.2 convolution_multiply_fusion.4
  132.4 1.2 convolution_multiply_fusion.6
  133.6 0.0 copy-done.1
  133.6 1.4 divide_bitcast_fusion
  135.0 1.4 divide_bitcast_fusion.1
  136.4 1.4 divide_bitcast_fusion.2
  137.8 1.4 divide_bitcast_fusion.3
  139.2 2.3 %pad_maximum_fusion = f32[4,256,1024]{2,1,0:T(8,128)} fusion(f32[1,256,1024]{2,1,0:T(8,128)S(1)} %get-tuple-element.19, f32[1,256,1024]{2,1,0:T(8,128)S(1)} %get-tuple-element.16, f32[1,256,1024]{2,1,0:T(8,128)S(1)} %get-tuple-element.13, f32[1,256,1024]{2,1,0:T(8,128)S(1)} %get-tuple-element.10), kind=kLoop, calls=%fused_computation.1 | loop fusion | flops 3145728 | bytes 8388608 | tf_op jit(solution)/shard_map/stack | solution.py:57
  141.5 2.6 %maximum_maximum_fusion = bf16[4,2,256,1024]{3,2,1,0:T(8,128)(2,1)} fusion(bf16[1,1,256,1024]{3,2,1,0:T(8,128)(2,1)S(1)} %get-tuple-element.21, bf16[1,1,256,1024]{3,2,1,0:T(8,128)(2,1)S(1)} %get-tuple-element.20, bf16[1,1,256,1024]{3,2,1,0:T(8,128)(2,1)S(1)} %get-tuple-element.18, bf16[1,1,256,1024]{3,2,1,0:T(8,128)(2,1)S(1)} %get-tuple-element.17, ...), kind=kLoop, calls=%fused_computation | loop fusion | flops 14680064 | bytes 8388608 | tf_op jit(solution)/shard_map/stack | solution.py:57
  (6 shorter events, 0.1 us)
Async XLA Ops:
  7.2 2.1 %copy-start = (bf16[256,512]{1,0:T(8,128)(2,1)S(1)}, bf16[256,512]{1,0:T(8,128)(2,1)}, u32[]{:S(2)}) copy-start(bf16[256,512]{1,0:T(8,128)(2,1)} %param.2) | copy-start | bytes 786436
  7.2 120.3 %all-gather.2.cloned.1.call-start = ((), (), s32[]{:S(2)}) async-start(), calls=%async_computation | async-start | bytes 4325376 | tf_op jit(solution)/shard_map/all_gather | solution.py:46
  48.5 85.2 %copy-start.1 = (bf16[256,256]{0,1:T(8,128)(2,1)S(1)}, bf16[256,256]{0,1:T(8,128)(2,1)}, u32[]{:S(2)}) copy-start(bf16[256,256]{0,1:T(8,128)(2,1)} %all-reduce.1) | copy-start | bytes 393220
Sparse Core Ops, SparseCore 0:
  48.6 78.7 all-gather.1
where the time goes:
time: 151 us
  waiting for transfers between devices  77.2 us (51%)
  blocking collectives  38.9 us (26%)
  between operations  14.2 us (9%)
  matrix products  10.7 us (7%)
  other arithmetic  9.9 us (7%)
    all_gather x1, waiting for transfers between devices, body(): gathered = lax.all_gather(spectra, 'svc', axis=0, tiled=True)  77.2 us
    psum x1, blocking collectives, body(): spectra = lax.psum(partial_value, 'tm').astype(jnp.bfloat16)  38.9 us
    dot_general x4, matrix products, band_products(): lax.dot_general(row_spec, col_spec, dims, preferred_element_type=jnp.floa...  5.53 us
    another operation x2, other arithmetic, body(): return (jnp.stack(cross_list, axis=0), jnp.stack(coherence_list, axis=0))  4.9 us
    dot_general x4, matrix products, band_products(): lax.dot_general(swapped, col_spec, dims, preferred_element_type=jnp.float32)  4.89 us
  transfers between devices with their start and end apart: 1, of which 1 were waited for; matrix products, arithmetic and copies ran while one was open for 1% of the time, Pallas kernels for 0%

commit v1 on v0

--- a/solution.py
+++ b/solution.py
@@ -40,7 +40,7 @@
     minutes = time_index * local_minutes + jnp.arange(local_minutes, dtype=jnp.int32)
     dft_table = make_table(minutes, band_starts)
     partial_value = jnp.dot(metrics, dft_table, preferred_element_type=jnp.float32)
-    spectra = lax.psum(partial_value, "tm").astype(jnp.bfloat16)
+    spectra = jnp.sum(lax.all_gather(partial_value, "tm"), axis=0).astype(jnp.bfloat16)
     owners = lax.axis_size("svc") // lax.axis_size("tm")
     col_count = row_count * owners
     gathered = lax.all_gather(spectra, "svc", axis=0, tiled=True)

time: 151 us -> 177 us (1.17)
  waiting for transfers between devices: 77.2 us -> 137 us
  blocking collectives: 38.9 us -> 0 us
  local copies, waits for them, and re-layouts: 0.01 us -> 2.48 us
    all_gather x0 -> x1, waiting for transfers between devices: none -> 66.3 us  [body(): lax.all_gather(partial_value, 'tm')]
    psum x1 -> x0, blocking collectives: 38.9 us -> none  [body(): spectra = lax.psum(partial_value, 'tm').astype(jnp.bfloat16)]
    all_gather x1, waiting for transfers between devices: 77.2 us -> 70.8 us  [body(): gathered = lax.all_gather(spectra, 'svc', axis=0, tiled=True)]
    unnamed x4 -> x5, local copies, waits for them, and re-layouts: 0.01 us -> 2.48 us
  transfers between devices with their start and end apart: 1 -> 2, of which waited for: 1 -> 2; matrix products, arithmetic and copies ran while one was open for 1% -> 1% of each run, Pallas kernels for 0% -> 0%
where the time goes in v1:
time: 177 us; the launch traced here: 176 us
  waiting for transfers between devices  137 us (77%)
  between operations  14.2 us (8%)
  matrix products  11.4 us (6%)
  other arithmetic  11.1 us (6%)
  local copies, waits for them, and re-layouts  2.48 us (1%)
    all_gather x1, waiting for transfers between devices, body(): gathered = lax.all_gather(spectra, 'svc', axis=0, tiled=True)  70.8 us
    all_gather x1, waiting for transfers between devices, body(): lax.all_gather(partial_value, 'tm')  66.3 us
    dot_general x4, matrix products, band_products(): lax.dot_general(row_spec, col_spec, dims, preferred_element_type=jnp.floa...  5.53 us
    another operation x2, other arithmetic, body(): return (jnp.stack(cross_list, axis=0), jnp.stack(coherence_list, axis=0))  4.9 us
    dot_general x4, matrix products, band_products(): lax.dot_general(swapped, col_spec, dims, preferred_element_type=jnp.float32)  4.89 us
  transfers between devices with their start and end apart: 2, of which 2 were waited for; matrix products, arithmetic and copies ran while one was open for 1% of the time, Pallas kernels for 0%

profile of v1, /device:TPU:1, one launch (start us, length us, event | category | flops | bytes accessed | tf_op | source)
XLA Modules:
  0.0 176.4 jit_solution(4841117717192794000)
XLA Ops:
  7.2 0.0 copy-start
  7.2 0.0 all-gather.6.cloned.1.call-start
  7.2 0.8 iota_add_fusion
  8.0 1.2 multiply_convert_fusion.1
  9.3 0.0 copy-done
  9.3 1.0 convolution_bitcast_fusion
  10.2 0.0 all-gather.6.cloned.1.call-update
  10.3 0.0 all-gather.4.cloned.1.call-start
  10.3 66.3 %all-gather.6.cloned.1.call-done = f32[2048,256]{0,1:T(8,128)} async-done(((f32[256,256]{0,1:T(8,128)}), f32[2048,256]{0,1:T(8,128)}) %all-gather.6.cloned.1.call-update) | async-done | bytes 2097168 | tf_op jit(solution)/shard_map/all_gather | solution.py:43
  76.6 2.5 %copy.4 = f32[32,8,8,256]{3,2,1,0:T(8,128)S(1)} copy(f32[32,8,8,256]{3,1,2,0:T(8,128)} %bitcast.34) | data formatting | bytes 4194304
  79.1 1.2 bitcast_reduce_fusion
  80.3 0.0 copy-start.1
  80.3 0.0 all-gather.4.cloned.1.call-update
  80.3 0.9 multiply_reduce_fusion.7
  81.2 0.9 fusion.33
  82.1 70.8 %all-gather.4.cloned.1.call-done = bf16[8192,256]{0,1:T(8,128)(2,1)} async-done(((bf16[256,256]{0,1:T(8,128)(2,1)}), bf16[8192,256]{0,1:T(8,128)(2,1)}) %all-gather.4.cloned.1.call-update) | async-done | bytes 4194320 | tf_op jit(solution)/shard_map/all_gather | solution.py:46
  152.9 1.2 multiply_reduce_fusion.3
  154.1 1.2 convolution_multiply_fusion
  155.4 1.2 convolution_multiply_fusion.2
  156.6 1.2 convolution_multiply_fusion.4
  157.8 1.2 convolution_multiply_fusion.6
  159.1 0.0 copy-done.1
  159.1 1.4 divide_bitcast_fusion
  160.5 1.4 divide_bitcast_fusion.1
  161.8 1.4 divide_bitcast_fusion.2
  163.2 1.4 divide_bitcast_fusion.3
  164.6 2.3 %pad_maximum_fusion = f32[4,256,1024]{2,1,0:T(8,128)} fusion(f32[1,256,1024]{2,1,0:T(8,128)S(1)} %get-tuple-element.19, f32[1,256,1024]{2,1,0:T(8,128)S(1)} %get-tuple-element.16, f32[1,256,1024]{2,1,0:T(8,128)S(1)} %get-tuple-element.13, f32[1,256,1024]{2,1,0:T(8,128)S(1)} %get-tuple-element.10), kind=kLoop, calls=%fused_computation.1 | loop fusion | flops 3145728 | bytes 8388608 | tf_op jit(solution)/shard_map/stack | solution.py:57
  167.0 2.6 %maximum_maximum_fusion = bf16[4,2,256,1024]{3,2,1,0:T(8,128)(2,1)} fusion(bf16[1,1,256,1024]{3,2,1,0:T(8,128)(2,1)S(1)} %get-tuple-element.21, bf16[1,1,256,1024]{3,2,1,0:T(8,128)(2,1)S(1)} %get-tuple-element.20, bf16[1,1,256,1024]{3,2,1,0:T(8,128)(2,1)S(1)} %get-tuple-element.18, bf16[1,1,256,1024]{3,2,1,0:T(8,128)(2,1)S(1)} %get-tuple-element.17, ...), kind=kLoop, calls=%fused_computation | loop fusion | flops 14680064 | bytes 8388608 | tf_op jit(solution)/shard_map/stack | solution.py:57
  (6 shorter events, 0.1 us)
Async XLA Ops:
  7.2 2.1 %copy-start = (bf16[256,512]{1,0:T(8,128)(2,1)S(1)}, bf16[256,512]{1,0:T(8,128)(2,1)}, u32[]{:S(2)}) copy-start(bf16[256,512]{1,0:T(8,128)(2,1)} %param.2) | copy-start | bytes 786436
  7.2 69.4 %all-gather.6.cloned.1.call-start = ((), (), s32[]{:S(2)}) async-start(), calls=%async_computation.1 | async-start | bytes 2359296 | tf_op jit(solution)/shard_map/all_gather | solution.py:43
  10.3 142.6 %all-gather.4.cloned.1.call-start = ((), (), s32[]{:S(2)}) async-start(), calls=%async_computation | async-start | bytes 4325376 | tf_op jit(solution)/shard_map/all_gather | solution.py:46
  80.3 78.8 %copy-start.1 = (bf16[256,256]{0,1:T(8,128)(2,1)S(1)}, bf16[256,256]{0,1:T(8,128)(2,1)}, u32[]{:S(2)}) copy-start(bf16[256,256]{0,1:T(8,128)(2,1)} %bitcast_reduce_fusion) | copy-start | bytes 393220
Sparse Core Ops, SparseCore 0:
  11.1 65.5 all-gather.5
  80.4 72.3 all-gather.3

commit v2 on v0

--- a/solution.py
+++ b/solution.py
@@ -43,7 +43,9 @@
     spectra = lax.psum(partial_value, "tm").astype(jnp.bfloat16)
     owners = lax.axis_size("svc") // lax.axis_size("tm")
     col_count = row_count * owners
-    gathered = lax.all_gather(spectra, "svc", axis=0, tiled=True)
+    gathered = jnp.concatenate(
+        lax.all_to_all(jnp.stack([spectra] * lax.axis_size("svc")), "svc", 0, 0), axis=0
+    )
     columns_panel = lax.dynamic_slice_in_dim(gathered, time_index * col_count, col_count, 0)
     cross_list = []
     coherence_list = []

time: 151 us -> 172 us (1.14)
  waiting for transfers between devices: 77.2 us -> 94.6 us
  starting transfers between devices: 0.04 us -> 16.8 us
  between operations: 14.2 us -> 0.86 us
  local copies, waits for them, and re-layouts: 0.01 us -> 10.8 us
  matrix products: 10.7 us -> 3.37 us
  other arithmetic: 9.9 us -> 7.17 us
    all_to_all x0 -> x1, waiting for transfers between devices: none -> 94.6 us  [body(): lax.all_to_all(jnp.stack([spectra] * lax.axis_size('svc')), 'svc', 0, 0)]
    all_gather x1 -> x0, waiting for transfers between devices: 77.2 us -> none  [body(): gathered = lax.all_gather(spectra, 'svc', axis=0, tiled=True)]
    all_to_all x0 -> x1, starting transfers between devices: none -> 16.8 us  [body(): lax.all_to_all(jnp.stack([spectra] * lax.axis_size('svc')), 'svc', 0, 0)]
    all_to_all x0 -> x1, local copies, waits for them, and re-layouts: none -> 6.4 us  [body(): lax.all_to_all(jnp.stack([spectra] * lax.axis_size('svc')), 'svc', 0, 0)]
    dot_general x4, matrix products: 5.53 us -> 1.8 us  [band_products(): lax.dot_general(row_spec, col_spec, dims, preferred_element_type=jnp.floa...]
    dot_general x4, matrix products: 4.89 us -> 1.3 us  [band_products(): lax.dot_general(swapped, col_spec, dims, preferred_element_type=jnp.float32)]
    another operation x0 -> x1, local copies, waits for them, and re-layouts: none -> 2.49 us  [body(): jnp.stack([spectra] * lax.axis_size('svc'))]
    unnamed x4 -> x7, local copies, waits for them, and re-layouts: 0.01 us -> 1.96 us
  transfers between devices with their start and end apart: 1 -> 1, of which waited for: 1 -> 1; matrix products, arithmetic and copies ran while one was open for 1% -> 0% of each run, Pallas kernels for 0% -> 0%
where the time goes in v2:
time: 172 us
  waiting for transfers between devices  94.6 us (55%)
  blocking collectives  38.4 us (22%)
  starting transfers between devices  16.8 us (10%)
  local copies, waits for them, and re-layouts  10.8 us (6%)
  other arithmetic  7.17 us (4%)
  matrix products  3.37 us (2%)
    all_to_all x1, waiting for transfers between devices, body(): lax.all_to_all(jnp.stack([spectra] * lax.axis_size('svc')), 'svc', 0, 0)  94.6 us
    psum x1, blocking collectives, body(): spectra = lax.psum(partial_value, 'tm').astype(jnp.bfloat16)  38.4 us
    all_to_all x1, starting transfers between devices, body(): lax.all_to_all(jnp.stack([spectra] * lax.axis_size('svc')), 'svc', 0, 0)  16.8 us
    all_to_all x1, local copies, waits for them, and re-layouts, body(): lax.all_to_all(jnp.stack([spectra] * lax.axis_size('svc')), 'svc', 0, 0)  6.4 us
    another operation x2, other arithmetic, body(): return (jnp.stack(cross_list, axis=0), jnp.stack(coherence_list, axis=0))  4.9 us
  transfers between devices with their start and end apart: 1, of which 1 were waited for; matrix products, arithmetic and copies ran while one was open for 0% of the time, Pallas kernels for 0%

profile of v2, /device:TPU:1, one launch (start us, length us, event | category | flops | bytes accessed | tf_op | source)
XLA Modules:
  0.0 172.0 jit_solution(16962961761272311974)
XLA Ops:
  0.6 0.0 copy-start
  0.7 0.8 iota_add_fusion
  1.4 1.2 multiply_convert_fusion.1
  2.7 0.0 copy-done
  2.7 0.3 convolution_bitcast_fusion
  3.0 38.4 %all-reduce.1 = bf16[256,256]{0,1:T(8,128)(2,1)S(1)} all-reduce(f32[256,256]{0,1:T(8,128)S(1)} %convolution_bitcast_fusion), channel_id=1, replica_groups=mesh['svc'=32,'tm'=8] {'tm'}, use_global_device_ids=true, to_apply=%region_0.1 | all-reduce | flops 65536 | bytes 393216 | tf_op jit(solution)/shard_map/psum | solution.py:43
  41.4 2.5 %stack.42 = bf16[32,256,256]{1,2,0:T(8,128)(2,1)} broadcast(bf16[256,256]{0,1:T(8,128)(2,1)S(1)} %all-reduce.1), dimensions={1,2} | broadcast | bytes 4325376 | tf_op jit(solution)/shard_map/stack | solution.py:47
  43.9 16.8 %all-to-all-start = ((bf16[32,256,256]{1,2,0:T(8,128)(2,1)}), bf16[32,256,256]{1,2,0:T(8,128)(2,1)}, u32[]{:S(2)}, u32[]{:S(2)}) async-start(bf16[32,256,256]{1,2,0:T(8,128)(2,1)} %stack.42), calls=%async_computation | async-start | bytes 8388608 | tf_op jit(solution)/shard_map/all_to_all | solution.py:47
  60.7 94.6 %all-to-all-done = bf16[32,256,256]{1,2,0:T(8,128)(2,1)} async-done(((bf16[32,256,256]{1,2,0:T(8,128)(2,1)}), bf16[32,256,256]{1,2,0:T(8,128)(2,1)}, u32[]{:S(2)}, u32[]{:S(2)}) %all-to-all-start) | async-done | bytes 4194336 | tf_op jit(solution)/shard_map/all_to_all | solution.py:47
  155.3 6.4 %copy.11 = bf16[32,256,256]{2,1,0:T(8,128)(2,1)} copy(bf16[32,256,256]{1,2,0:T(8,128)(2,1)} %all-to-all-done) | data formatting | bytes 8388608 | tf_op jit(solution)/shard_map/all_to_all | solution.py:47
  161.7 1.4 constant_dynamic-slice_fusion
  163.2 0.1 copy.14
  163.3 0.1 copy.16
  163.5 0.1 copy.15
  163.7 0.1 copy.17
  163.9 0.3 convolution_multiply_fusion.6
  164.3 0.3 convolution_multiply_fusion.2
  164.6 0.3 convolution_multiply_fusion.4
  164.9 0.3 convolution_multiply_fusion
  165.2 0.5 divide_bitcast_fusion.3
  165.7 0.5 divide_bitcast_fusion.1
  166.2 0.4 divide_bitcast_fusion.2
  166.6 0.5 divide_bitcast_fusion
  167.1 2.3 %pad_maximum_fusion = f32[4,256,1024]{2,1,0:T(8,128)} fusion(f32[1,256,1024]{2,1,0:T(8,128)S(1)} %get-tuple-element.19, f32[1,256,1024]{2,1,0:T(8,128)S(1)} %get-tuple-element.16, f32[1,256,1024]{2,1,0:T(8,128)S(1)} %get-tuple-element.13, f32[1,256,1024]{2,1,0:T(8,128)S(1)} %get-tuple-element.10), kind=kLoop, calls=%fused_computation.1 | loop fusion | flops 3145728 | bytes 8388608 | tf_op jit(solution)/shard_map/stack | solution.py:59
  169.4 2.6 %maximum_maximum_fusion = bf16[4,2,256,1024]{3,2,1,0:T(8,128)(2,1)} fusion(bf16[1,1,256,1024]{3,2,1,0:T(8,128)(2,1)S(1)} %get-tuple-element.21, bf16[1,1,256,1024]{3,2,1,0:T(8,128)(2,1)S(1)} %get-tuple-element.20, bf16[1,1,256,1024]{3,2,1,0:T(8,128)(2,1)S(1)} %get-tuple-element.18, bf16[1,1,256,1024]{3,2,1,0:T(8,128)(2,1)S(1)} %get-tuple-element.17, ...), kind=kLoop, calls=%fused_computation | loop fusion | flops 14680064 | bytes 8388608 | tf_op jit(solution)/shard_map/stack | solution.py:59
  (14 shorter events, 0.3 us)
Async XLA Ops:
  0.6 2.1 %copy-start = (bf16[256,512]{1,0:T(8,128)(2,1)S(1)}, bf16[256,512]{1,0:T(8,128)(2,1)}, u32[]{:S(2)}) copy-start(bf16[256,512]{1,0:T(8,128)(2,1)} %param.2) | copy-start | bytes 786436
  43.9 111.4 %all-to-all-start = ((bf16[32,256,256]{1,2,0:T(8,128)(2,1)}), bf16[32,256,256]{1,2,0:T(8,128)(2,1)}, u32[]{:S(2)}, u32[]{:S(2)}) async-start(bf16[32,256,256]{1,2,0:T(8,128)(2,1)} %stack.42), calls=%async_computation | async-start | bytes 8388608 | tf_op jit(solution)/shard_map/all_to_all | solution.py:47
